TPU v7x, 32 devices: a whole 2x2x4 slice. The times are simulated.
32 devices in a mesh: gz: 4 (over x, core), gy: 4 (over z), gx: 2 (over y).
Axes of the slice: x: 2, y: 2, z: 4, core: 2. Of those that a mesh axis runs over, the one named last changes fastest.
Arguments:
- volume: bfloat16 [32, 4, 32, 384], P('gz', 'gy', 'gx'), may hold values from -80 to 80
- cotangent: bfloat16 [32, 4, 32, 384], P('gz', 'gy', 'gx'), may hold values from -6 to 6
- w_project: bfloat16 [3, 384, 1152], P(None, 'gy', ('gz', 'gx')), may hold values from -0.3125 to 0.3125
- w_output: bfloat16 [3, 384, 384], P(None, 'gy', ('gz', 'gx')), may hold values from -0.3125 to 0.3125
Outputs:
- grad_volume: bfloat16 [32, 4, 32, 384], P('gz', 'gy', 'gx')
All inputs are finite; a program needn't handle non-finite values.
Results may differ from a plain program's by a relative error of at most 0.015.
Values may be sent and summed in bfloat16 or wider, within the bound.
No kernel may reach another device: no remote copies, remote signals or barrier semaphores. Data moves between devices by JAX's collectives and lax.ppermute only.
A program may use at most 64 MiB of HBM per device.

v0:
```python
import jax
import jax.numpy as jnp
from jax import lax
from jax.sharding import PartitionSpec as P

HEADS = 6
HIGHEST = lax.Precision.HIGHEST
ALL = ("gz", "gy", "gx")


def head_map(feat_len):
    head_size = feat_len // HEADS
    return (jnp.arange(feat_len)[:, None] // head_size == jnp.arange(HEADS)[None, :]).astype(
        jnp.float32
    )


def head_norm(vector, ones):
    head_size = vector.shape[-1] // HEADS
    sums = jnp.dot(vector * vector, ones, precision=lax.Precision.HIGH)
    scale = lax.rsqrt(sums / head_size + 1e-06)
    return (vector * jnp.dot(scale, ones.T, precision=lax.Precision.HIGH)).astype(jnp.bfloat16)


def sublayer(line_rows, w_inner, w_outer):
    feat_len = line_rows.shape[-1]
    head_size = feat_len // HEADS
    ones = head_map(feat_len)
    mask = ones.T.astype(jnp.bfloat16)
    stream = line_rows.astype(jnp.float32)
    normed = (stream * lax.rsqrt(jnp.mean(stream * stream, axis=-1, keepdims=True) + 1e-06)).astype(
        jnp.bfloat16
    )
    packed = jnp.dot(normed, w_inner, preferred_element_type=jnp.float32)
    queries = head_norm(packed[..., :feat_len], ones)
    key_part = head_norm(packed[..., feat_len : 2 * feat_len], ones)
    value_part = packed[..., 2 * feat_len :].astype(jnp.bfloat16)
    if line_rows.shape[1] <= 8:
        pairs = queries[:, :, None].astype(jnp.float32) * key_part[:, None].astype(jnp.float32)
        scores = jnp.dot(pairs, ones, precision=lax.Precision.HIGH) * head_size ** (-0.5)
        powers = jnp.exp(scores)
        attn_weights = (powers / jnp.sum(powers, axis=2, keepdims=True)).astype(jnp.bfloat16)
        spread = jnp.dot(attn_weights, mask, preferred_element_type=jnp.float32)
        mixed_out = jnp.sum(spread * value_part[:, None].astype(jnp.float32), axis=2).astype(
            jnp.bfloat16
        )
    else:
        key_heads = key_part[..., None, :] * mask
        scores = jnp.einsum(
            "plqd,pkqhd->pqhlk", queries, key_heads, preferred_element_type=jnp.float32
        ) * head_size ** (-0.5)
        powers = jnp.exp(scores)
        attn_weights = (powers / jnp.sum(powers, axis=-1, keepdims=True)).astype(jnp.bfloat16)
        mixed_heads = jnp.einsum(
            "pqhlk,pkqd->plqhd", attn_weights, value_part, preferred_element_type=jnp.float32
        )
        mixed_out = jnp.sum(mixed_heads * mask.astype(jnp.float32), axis=-2).astype(jnp.bfloat16)
    update = jnp.dot(mixed_out, w_outer, preferred_element_type=jnp.float32)
    return (stream + update).astype(jnp.bfloat16)


def full_weights(w_project, w_output, sizes):
    subs, din, dproj = w_project.shape
    ny = sizes[1]
    source = (lax.axis_index("gy") - jnp.arange(ny)) % ny

    def over_gy(block):
        shifted = [block] + [
            lax.ppermute(block, "gy", [(i, (i + s) % ny) for i in range(ny)]) for s in range(1, ny)
        ]
        rows = jnp.take(jnp.stack(shifted), source, axis=0)
        return jnp.swapaxes(rows, 0, 1).reshape(subs, ny * din, block.shape[2])

    proj = lax.all_gather(over_gy(w_project), ("gz", "gx"), axis=2, tiled=True)
    outp = lax.all_gather(over_gy(w_output), ("gz", "gx"), axis=2, tiled=True)
    return [(proj[i], outp[i]) for i in range(subs)]


def depth_fn(member, w_inner, w_outer):
    depth_len, row_len, rest_len, feat_len = member.shape
    flat_lines = member.reshape(1, depth_len, row_len * rest_len, feat_len)
    return sublayer(flat_lines, w_inner, w_outer).reshape(member.shape)


def plane_fn(plane, w_row, w_col):
    after_rows = sublayer(plane[None], *w_row)[0]
    return sublayer(after_rows[:, :, None, :], *w_col)[:, :, 0, :]


def to_planes(depth_lines, sizes):
    nz, ny, nx = sizes
    z_len, yl, kx, feat = depth_lines.shape
    got = lax.all_to_all(depth_lines, ALL, 0, 0, tiled=True)
    got = got.reshape(nz, ny, nx, yl, kx, feat)
    return jnp.transpose(got, (1, 3, 2, 0, 4, 5)).reshape(ny * yl, nx * nz * kx, feat)


def from_planes(plane, sizes):
    nz, ny, nx = sizes
    rows, cols, feat = plane.shape
    yl, kx = (rows // ny, cols // (nx * nz))
    parts = plane.reshape(ny, yl, nx, nz, kx, feat)
    parts = jnp.transpose(parts, (3, 0, 2, 1, 4, 5)).reshape(nz * ny * nx, yl, kx, feat)
    return lax.all_to_all(parts, ALL, 0, 0, tiled=True)


def block_to_plane(block, sizes):
    nz, ny, nx = sizes
    zl, yl, xl, feat = block.shape
    got = lax.all_to_all(block, ("gy", "gx"), 0, 0, tiled=True)
    got = got.reshape(ny, nx, yl, xl, feat)
    return jnp.transpose(got, (0, 2, 1, 3, 4)).reshape(ny * yl, nx * xl, feat)


def local(volume, cotangent, w_project, w_output, sizes):
    w_depth, w_row, w_col = full_weights(w_project, w_output, sizes)
    depth_act = lax.all_to_all(volume, "gz", 2, 0, tiled=True)
    cot_plane = block_to_plane(cotangent, sizes)
    field_one, depth_pullback = jax.vjp(lambda m: depth_fn(m, *w_depth), depth_act)
    plane_one = to_planes(field_one, sizes)
    _, plane_pullback = jax.vjp(lambda p: plane_fn(p, w_row, w_col), plane_one)
    grad_plane = plane_pullback(cot_plane)[0]
    grad_one = from_planes(grad_plane, sizes)
    grad_zero = depth_pullback(grad_one)[0]
    return lax.all_to_all(grad_zero, "gz", 0, 2, tiled=True)


def along_rows(member, w_inner, w_outer):
    return sublayer(member, w_inner, w_outer)


def along_columns(member, w_inner, w_outer):
    depth_len, row_len, col_len, feat_len = member.shape
    flat_lines = member.reshape(depth_len * row_len, col_len, 1, feat_len)
    return sublayer(flat_lines, w_inner, w_outer).reshape(member.shape)


def line_swap(stacked, axis, split_axis, concat_axis):
    return lax.all_to_all(stacked, axis, split_axis=split_axis, concat_axis=concat_axis, tiled=True)


def local_general(volume, cotangent, w_project, w_output, sizes):
    w_depth, w_row, w_col = full_weights(w_project, w_output, sizes)

    def row_fn(member):
        return along_rows(member, *w_row)

    def column_fn(member):
        return along_columns(member, *w_col)

    depth_act = line_swap(volume, "gz", 2, 0)
    field_one, depth_pullback = jax.vjp(lambda m: depth_fn(m, *w_depth), depth_act)
    field_one = line_swap(field_one, "gz", 0, 2)
    row_act = line_swap(field_one, "gy", 2, 1)
    field_two, row_pullback = jax.vjp(row_fn, row_act)
    field_two = line_swap(field_two, "gy", 1, 2)
    paired = line_swap(jnp.stack([cotangent, field_two]), "gx", 1, 3)
    _, column_pullback = jax.vjp(column_fn, paired[1])
    grad_two = line_swap(column_pullback(paired[0])[0], "gx", 2, 0)
    grad_one = line_swap(row_pullback(line_swap(grad_two, "gy", 2, 1))[0], "gy", 1, 2)
    grad_zero = depth_pullback(line_swap(grad_one, "gz", 2, 0))[0]
    return line_swap(grad_zero, "gz", 0, 2)


def solution(mesh):
    sizes = (mesh.shape["gz"], mesh.shape["gy"], mesh.shape["gx"])

    def body(volume, *rest):
        one_depth = volume.shape[0] * sizes[0] == mesh.size
        return (local if one_depth else local_general)(volume, *rest, sizes)

    return jax.shard_map(
        body,
        mesh=mesh,
        in_specs=(
            P("gz", "gy", "gx", None),
            P("gz", "gy", "gx", None),
            P(None, "gy", ("gz", "gx")),
            P(None, "gy", ("gz", "gx")),
        ),
        out_specs=P("gz", "gy", "gx", None),
        check_vma=False,
    )
```

profile of v0, /device:TPU:0, one launch (start us, length us, event | category | flops | bytes accessed | tf_op | source)
XLA Modules:
  0.0 132.1 jit_solution(2418500151631006704)
XLA Ops:
  6.5 3.1 %collective-permute-start.3 = (bf16[3,96,144]{1,2,0:T(8,128)(2,1)}, bf16[3,96,144]{1,2,0:T(8,128)(2,1)S(1)}, u32[]{:S(2)}, u32[]{:S(2)}) collective-permute-start(bf16[3,96,144]{1,2,0:T(8,128)(2,1)} %param.6), channel_id=1, source_target_pairs={{0,2},{2,4},{4,6},{6,0},{1,3},{3,5},{5,7},{7,1},{8,10},{10,12},{12... | collective-permute-start | bytes 248840 | tf_op jit(solution)/shard_map/ppermute | solution.py:69
  9.6 2.6 %collective-permute-start.4 = (bf16[3,96,144]{1,2,0:T(8,128)(2,1)}, bf16[3,96,144]{1,2,0:T(8,128)(2,1)S(1)}, u32[]{:S(2)}, u32[]{:S(2)}) collective-permute-start(bf16[3,96,144]{1,2,0:T(8,128)(2,1)} %param.6), channel_id=1, source_target_pairs={{0,4},{2,6},{4,0},{6,2},{1,5},{3,7},{5,1},{7,3},{8,12},{10,14},{12... | collective-permute-start | bytes 248840 | tf_op jit(solution)/shard_map/ppermute | solution.py:69
  12.2 1.3 %collective-permute-start.5 = (bf16[3,96,144]{1,2,0:T(8,128)(2,1)}, bf16[3,96,144]{1,2,0:T(8,128)(2,1)S(1)}, u32[]{:S(2)}, u32[]{:S(2)}) collective-permute-start(bf16[3,96,144]{1,2,0:T(8,128)(2,1)} %param.6), channel_id=1, source_target_pairs={{0,6},{2,0},{4,2},{6,4},{1,7},{3,1},{5,3},{7,5},{8,14},{10,8},{12,... | collective-permute-start | bytes 248840 | tf_op jit(solution)/shard_map/ppermute | solution.py:69
  13.6 2.3 %collective-permute-done.3 = bf16[3,96,144]{1,2,0:T(8,128)(2,1)S(1)} collective-permute-done((bf16[3,96,144]{1,2,0:T(8,128)(2,1)}, bf16[3,96,144]{1,2,0:T(8,128)(2,1)S(1)}, u32[]{:S(2)}, u32[]{:S(2)}) %collective-permute-start.3) | collective-permute-done | bytes 82976 | tf_op jit(solution)/shard_map/ppermute | solution.py:69
  15.8 3.9 %collective-permute-done.4 = bf16[3,96,144]{1,2,0:T(8,128)(2,1)S(1)} collective-permute-done((bf16[3,96,144]{1,2,0:T(8,128)(2,1)}, bf16[3,96,144]{1,2,0:T(8,128)(2,1)S(1)}, u32[]{:S(2)}, u32[]{:S(2)}) %collective-permute-start.4) | collective-permute-done | bytes 82976 | tf_op jit(solution)/shard_map/ppermute | solution.py:69
  19.7 1.0 pad_maximum_fusion
  20.8 0.6 gather_fusion.1
  21.7 1.0 reshape.892
  22.8 2.9 %collective-permute-start = (bf16[3,96,48]{1,2,0:T(8,128)(2,1)S(1)}, bf16[3,96,48]{1,2,0:T(8,128)(2,1)S(1)}, u32[]{:S(2)}, u32[]{:S(2)}) collective-permute-start(bf16[3,96,48]{1,2,0:T(8,128)(2,1)S(1)} %copy-done.15), channel_id=1, source_target_pairs={{0,2},{2,4},{4,6},{6,0},{1,3},{3,5},{5,7},{7,1},{8,10},{10,12},{12... | collective-permute-start | bytes 82952 | tf_op jit(solution)/shard_map/ppermute | solution.py:69
  25.7 1.6 %collective-permute-start.1 = (bf16[3,96,48]{1,2,0:T(8,128)(2,1)S(1)}, bf16[3,96,48]{1,2,0:T(8,128)(2,1)S(1)}, u32[]{:S(2)}, u32[]{:S(2)}) collective-permute-start(bf16[3,96,48]{1,2,0:T(8,128)(2,1)S(1)} %copy-done.15), channel_id=1, source_target_pairs={{0,4},{2,6},{4,0},{6,2},{1,5},{3,7},{5,1},{7,3},{8,12},{10,14},{12... | collective-permute-start | bytes 82952 | tf_op jit(solution)/shard_map/ppermute | solution.py:69
  27.3 0.8 collective-permute-start.2
  28.1 0.7 copy.78
  28.8 3.3 %all-to-all-start.1 = ((bf16[8,1,16,384]{3,0,1,2:T(8,128)(2,1)}), bf16[8,1,16,384]{3,0,1,2:T(8,128)(2,1)S(1)}, u32[]{:S(2)}, u32[]{:S(2)}) async-start(bf16[8,1,16,384]{3,0,1,2:T(8,128)(2,1)} %copy.78), calls=%async_computation.1 | async-start | bytes 196608 | tf_op jit(solution)/shard_map/all_to_all | solution.py:117
  32.2 0.6 gather_fusion
  33.1 22.7 %all_gather.6 = bf16[3,384,384]{1,2,0:T(8,128)(2,1)S(1)} all-gather(bf16[3,384,48]{1,2,0:T(8,128)(2,1)S(1)} %reshape.890), channel_id=1, replica_groups=mesh['gz'=4,'gy'=4,'gx'=2] {'gz','gx'}, dimensions={2}, use_global_device_ids=true | all-gather | bytes 995328 | tf_op jit(solution)/shard_map/all_gather | solution.py:75
  55.8 4.9 %all-to-all-start = ((bf16[8,1,16,384]{3,2,1,0:T(8,128)(2,1)}), bf16[8,1,16,384]{3,2,1,0:T(8,128)(2,1)S(1)}, u32[]{:S(2)}, u32[]{:S(2)}) async-start(bf16[8,1,16,384]{3,2,1,0:T(8,128)(2,1)} %param.5), calls=%async_computation | async-start | bytes 196608 | tf_op jit(solution)/shard_map/all_to_all | solution.py:110
  60.9 0.7 add.159
  61.5 1.6 %convolution_bitcast_fusion.2 = f32[1,32,4,1152]{3,1,2,0:T(8,128)S(1)} fusion(bf16[3,384,1152]{1,2,0:T(8,128)(2,1)} %all-gather.2.cloned.1.call-done, bf16[8,1,4,4,384]{4,0,3,2,1:T(8,128)(2,1)S(1)} %bitcast.588, f32[4,8,4]{1,2,0:T(4,128)S(1)} %get-tuple-element.16), kind=kOutput, calls=%fused_computation.4 | convolution fusion | flops 113393664 | bytes 1573376 | tf_op jit(solution)/shard_map/jvp()/dot_general | solution.py:34
  65.6 0.4 fusion.1
  66.3 0.7 copy.86
  67.0 1.3 all-to-all-done
  68.3 4.8 %all-to-all-start.2 = ((bf16[32,1,4,384]{3,2,1,0:T(4,128)(2,1)}), bf16[32,1,4,384]{3,2,1,0:T(4,128)(2,1)S(1)}, u32[]{:S(2)}, u32[]{:S(2)}) async-start(bf16[32,1,4,384]{3,2,1,0:T(4,128)(2,1)} %copy.86), calls=%async_computation.2 | async-start | bytes 196608 | tf_op jit(solution)/shard_map/all_to_all | solution.py:93
  73.3 7.4 %all-to-all-done.2 = bf16[32,1,4,384]{3,2,1,0:T(4,128)(2,1)S(1)} async-done(((bf16[32,1,4,384]{3,2,1,0:T(4,128)(2,1)}), bf16[32,1,4,384]{3,2,1,0:T(4,128)(2,1)S(1)}, u32[]{:S(2)}, u32[]{:S(2)}) %all-to-all-start.2) | async-done | bytes 98336 | tf_op jit(solution)/shard_map/all_to_all | solution.py:93
  80.8 0.6 multiply_add_fusion
  81.5 1.6 %convolution_bitcast_fusion.1 = f32[1,4,32,1152]{3,2,1,0:T(8,128)S(1)} fusion(bf16[4,32,384]{2,1,0:T(8,128)(2,1)S(1)} %convert_element_type.547, bf16[3,384,1152]{1,2,0:T(8,128)(2,1)} %all-gather.2.cloned.1.call-done), kind=kOutput, calls=%fused_computation.3 | convolution fusion | flops 113246208 | bytes 1572864 | tf_op jit(solution)/shard_map/jvp()/dot_general | solution.py:34
  83.7 0.7 copy_bitcast_fusion
  84.7 1.0 reshape.923
  85.7 1.0 fusion.204
  86.7 0.8 fusion.335
  88.2 0.4 convolution_bitcast_fusion
  90.4 0.7 fusion.129
  92.9 0.4 multiply_reduce_fusion.5
  93.7 0.7 multiply_reduce_fusion.2
  94.4 0.4 multiply_reduce_fusion.9
  94.9 0.5 multiply_reduce_fusion.1
  96.0 0.9 fusion.80
  96.9 1.4 %add.158 = f32[4,32]{1,0:T(4,128)} reshape(f32[4,2,4,4]{3,2,1,0:T(4,128)} %get-tuple-element.13) | data formatting | bytes 1024 | tf_op jit(solution)/shard_map/jvp()/add | solution.py:31
  98.3 1.0 add_add_fusion.4
  99.3 1.6 %multiply_reduce_fusion.4 = (f32[4,32]{1,0:T(4,128)S(1)}, f32[4,32,384]{2,1,0:T(8,128)S(1)}) fusion(f32[4,32,384]{2,1,0:T(8,128)S(1)} %reshape.923, bf16[3,384,1152]{1,2,0:T(8,128)(2,1)} %all-gather.2.cloned.1.call-done, f32[1,4,32,384]{3,2,1,0:T(8,128)S(1)} %add_add_fusion.4, f32[1,4,32,384]{3,2,1,0:T(8,128)S(1)} %add_add_fusion.5, ...), kind=kOutput, calls=%fused_computation.248 | convolution fusion | flops 113885056 | bytes 1769984 | tf_op jit(solution)/shard_map/transpose(jvp())/dot_general | solution.py:34
  101.2 0.7 copy.92
  101.8 2.7 %all-to-all-start.3 = ((bf16[32,1,4,384]{3,2,1,0:T(4,128)(2,1)}), bf16[32,1,4,384]{3,2,1,0:T(4,128)(2,1)S(1)}, u32[]{:S(2)}, u32[]{:S(2)}) async-start(bf16[32,1,4,384]{3,2,1,0:T(4,128)(2,1)} %bitcast.118), calls=%async_computation.3 | async-start | bytes 196608 | tf_op jit(solution)/shard_map/all_to_all | solution.py:104
  104.6 7.4 %all-to-all-done.3 = bf16[32,1,4,384]{3,2,1,0:T(4,128)(2,1)S(1)} async-done(((bf16[32,1,4,384]{3,2,1,0:T(4,128)(2,1)}), bf16[32,1,4,384]{3,2,1,0:T(4,128)(2,1)S(1)}, u32[]{:S(2)}, u32[]{:S(2)}) %all-to-all-start.3) | async-done | bytes 98336 | tf_op jit(solution)/shard_map/all_to_all | solution.py:104
  112.5 0.7 fusion.125
  113.6 0.5 copy-done.12
  114.4 0.4 copy-done.7
  116.1 1.6 %fusion.181 = (f32[32,4]{0,1:T(4,128)S(1)}, f32[32,4,384]{2,0,1:T(8,128)S(1)}) fusion(bf16[3,384,1152]{1,2,0:T(8,128)(2,1)} %all-gather.2.cloned.1.call-done, f32[1,32,4,384]{3,1,2,0:T(8,128)S(1)} %add_add_fusion.1, f32[1,32,4,384]{3,1,2,0:T(8,128)S(1)} %add_add_fusion.2, bf16[1,32,4,384]{3,1,2,0:T(8,128)(2,1)S(1)} %fusion.72, ...), kind=kOutput, calls=%fused_computation.245 | convolution fusion | flops 113934208 | bytes 1671680 | tf_op jit(solution)/shard_map/transpose(jvp())/dot_general | solution.py:34
  117.9 6.7 %all_to_all.42 = bf16[32,1,4,384]{3,2,1,0:T(4,128)(2,1)S(1)} all-to-all(bf16[32,1,4,384]{3,2,1,0:T(4,128)(2,1)S(1)} %copy.96), channel_id=1, replica_groups=mesh['gz'=4,'gy'=4,'gx'=2] {'gz'}, dimensions={0} | all-to-all | bytes 196608 | tf_op jit(solution)/shard_map/all_to_all | solution.py:125
  124.6 0.7 all_to_all.36
  (121 shorter events, 12.6 us)
Async XLA Ops:
  6.5 55.0 %all-gather.2.cloned.1.call-start = ((), (), s32[]{:S(2)}) async-start(), calls=%async_computation.5 | async-start | bytes 2985984 | tf_op jit(solution)/shard_map/all_gather | solution.py:74
  6.5 9.3 %collective-permute-start.3 = (bf16[3,96,144]{1,2,0:T(8,128)(2,1)}, bf16[3,96,144]{1,2,0:T(8,128)(2,1)S(1)}, u32[]{:S(2)}, u32[]{:S(2)}) collective-permute-start(bf16[3,96,144]{1,2,0:T(8,128)(2,1)} %param.6), channel_id=1, source_target_pairs={{0,2},{2,4},{4,6},{6,0},{1,3},{3,5},{5,7},{7,1},{8,10},{10,12},{12... | collective-permute-start | bytes 248840 | tf_op jit(solution)/shard_map/ppermute | solution.py:69
  9.6 10.1 %collective-permute-start.4 = (bf16[3,96,144]{1,2,0:T(8,128)(2,1)}, bf16[3,96,144]{1,2,0:T(8,128)(2,1)S(1)}, u32[]{:S(2)}, u32[]{:S(2)}) collective-permute-start(bf16[3,96,144]{1,2,0:T(8,128)(2,1)} %param.6), channel_id=1, source_target_pairs={{0,4},{2,6},{4,0},{6,2},{1,5},{3,7},{5,1},{7,3},{8,12},{10,14},{12... | collective-permute-start | bytes 248840 | tf_op jit(solution)/shard_map/ppermute | solution.py:69
  12.2 7.5 %collective-permute-start.5 = (bf16[3,96,144]{1,2,0:T(8,128)(2,1)}, bf16[3,96,144]{1,2,0:T(8,128)(2,1)S(1)}, u32[]{:S(2)}, u32[]{:S(2)}) collective-permute-start(bf16[3,96,144]{1,2,0:T(8,128)(2,1)} %param.6), channel_id=1, source_target_pairs={{0,6},{2,0},{4,2},{6,4},{1,7},{3,1},{5,3},{7,5},{8,14},{10,8},{12,... | collective-permute-start | bytes 248840 | tf_op jit(solution)/shard_map/ppermute | solution.py:69
  21.5 1.3 copy-start.15
  21.5 6.6 %copy-start.10 = (bf16[8,1,16,384]{3,2,1,0:T(8,128)(2,1)S(1)}, bf16[8,1,16,384]{3,2,1,0:T(8,128)(2,1)}, u32[]{:S(2)}) copy-start(bf16[8,1,16,384]{3,2,1,0:T(8,128)(2,1)} %param.4) | copy-start | bytes 294916
  22.8 9.3 %collective-permute-start = (bf16[3,96,48]{1,2,0:T(8,128)(2,1)S(1)}, bf16[3,96,48]{1,2,0:T(8,128)(2,1)S(1)}, u32[]{:S(2)}, u32[]{:S(2)}) collective-permute-start(bf16[3,96,48]{1,2,0:T(8,128)(2,1)S(1)} %copy-done.15), channel_id=1, source_target_pairs={{0,2},{2,4},{4,6},{6,0},{1,3},{3,5},{5,7},{7,1},{8,10},{10,12},{12... | collective-permute-start | bytes 82952 | tf_op jit(solution)/shard_map/ppermute | solution.py:69
  25.7 6.5 %collective-permute-start.1 = (bf16[3,96,48]{1,2,0:T(8,128)(2,1)S(1)}, bf16[3,96,48]{1,2,0:T(8,128)(2,1)S(1)}, u32[]{:S(2)}, u32[]{:S(2)}) collective-permute-start(bf16[3,96,48]{1,2,0:T(8,128)(2,1)S(1)} %copy-done.15), channel_id=1, source_target_pairs={{0,4},{2,6},{4,0},{6,2},{1,5},{3,7},{5,1},{7,3},{8,12},{10,14},{12... | collective-permute-start | bytes 82952 | tf_op jit(solution)/shard_map/ppermute | solution.py:69
  27.3 4.9 %collective-permute-start.2 = (bf16[3,96,48]{1,2,0:T(8,128)(2,1)S(1)}, bf16[3,96,48]{1,2,0:T(8,128)(2,1)S(1)}, u32[]{:S(2)}, u32[]{:S(2)}) collective-permute-start(bf16[3,96,48]{1,2,0:T(8,128)(2,1)S(1)} %copy-done.15), channel_id=1, source_target_pairs={{0,6},{2,0},{4,2},{6,4},{1,7},{3,1},{5,3},{7,5},{8,14},{10,8},{12,... | collective-permute-start | bytes 82952 | tf_op jit(solution)/shard_map/ppermute | solution.py:69
  28.8 27.1 %all-to-all-start.1 = ((bf16[8,1,16,384]{3,0,1,2:T(8,128)(2,1)}), bf16[8,1,16,384]{3,0,1,2:T(8,128)(2,1)S(1)}, u32[]{:S(2)}, u32[]{:S(2)}) async-start(bf16[8,1,16,384]{3,0,1,2:T(8,128)(2,1)} %copy.78), calls=%async_computation.1 | async-start | bytes 196608 | tf_op jit(solution)/shard_map/all_to_all | solution.py:117
  32.1 59.4 %copy-start.20 = (bf16[6,384]{1,0:T(8,128)(2,1)}, bf16[6,384]{1,0:T(8,128)(2,1)S(1)}, u32[]{:S(2)}) copy-start(bf16[6,384]{1,0:T(8,128)(2,1)S(1)} %get-tuple-element.22) | copy-start | bytes 13828
  55.8 12.4 %all-to-all-start = ((bf16[8,1,16,384]{3,2,1,0:T(8,128)(2,1)}), bf16[8,1,16,384]{3,2,1,0:T(8,128)(2,1)S(1)}, u32[]{:S(2)}, u32[]{:S(2)}) async-start(bf16[8,1,16,384]{3,2,1,0:T(8,128)(2,1)} %param.5), calls=%async_computation | async-start | bytes 196608 | tf_op jit(solution)/shard_map/all_to_all | solution.py:110
  63.4 0.6 copy-start.6
  64.0 0.6 copy-start.8
  65.0 0.6 copy-start.11
  65.0 1.0 copy-start.13
  65.3 0.9 copy-start.2
  65.3 0.9 copy-start.16
  68.3 12.4 %all-to-all-start.2 = ((bf16[32,1,4,384]{3,2,1,0:T(4,128)(2,1)}), bf16[32,1,4,384]{3,2,1,0:T(4,128)(2,1)S(1)}, u32[]{:S(2)}, u32[]{:S(2)}) async-start(bf16[32,1,4,384]{3,2,1,0:T(4,128)(2,1)} %copy.86), calls=%async_computation.2 | async-start | bytes 196608 | tf_op jit(solution)/shard_map/all_to_all | solution.py:93
  83.7 3.8 %copy-start.4 = (f32[4,32,6]{1,2,0:T(8,128)}, f32[4,32,6]{1,2,0:T(8,128)S(1)}, u32[]{:S(2)}) copy-start(f32[4,32,6]{1,2,0:T(8,128)S(1)} %fusion.87) | copy-start | bytes 9220
  85.7 2.5 %copy-start = (bf16[3,384,1152]{1,2,0:T(8,128)(2,1)S(1)}, bf16[3,384,1152]{1,2,0:T(8,128)(2,1)}, u32[]{:S(2)}) copy-start(bf16[3,384,1152]{1,2,0:T(8,128)(2,1)} %all-gather.2.cloned.1.call-done) | copy-start | bytes 7962628
  94.9 1.2 copy-start.5
  94.9 3.4 %copy-start.1 = (f32[4,32,384]{2,1,0:T(8,128)S(1)}, f32[4,32,384]{2,1,0:T(8,128)}, u32[]{:S(2)}) copy-start(f32[4,32,384]{2,1,0:T(8,128)} %get-tuple-element.25) | copy-start | bytes 589828
  99.3 1.7 %copy-start.19 = (f32[4,32]{1,0:T(4,128)S(1)}, f32[4,32]{1,0:T(4,128)}, u32[]{:S(2)}) copy-start(f32[4,32]{1,0:T(4,128)} %add.158) | copy-start | bytes 1540
  99.3 5.3 %copy-start.17 = (f32[4,6,32]{2,1,0:T(8,128)S(1)}, f32[4,6,32]{2,1,0:T(8,128)}, u32[]{:S(2)}) copy-start(f32[4,6,32]{2,1,0:T(8,128)} %copy-done.16) | copy-start | bytes 9220
  101.0 11.2 %copy-start.3 = (f32[1,4,6,32,32]{3,4,2,1,0:T(8,128)S(1)}, f32[1,4,6,32,32]{3,4,2,1,0:T(8,128)}, u32[]{:S(2)}) copy-start(f32[1,4,6,32,32]{3,4,2,1,0:T(8,128)} %copy-done.2) | copy-start | bytes 294916
  101.8 10.2 %all-to-all-start.3 = ((bf16[32,1,4,384]{3,2,1,0:T(4,128)(2,1)}), bf16[32,1,4,384]{3,2,1,0:T(4,128)(2,1)S(1)}, u32[]{:S(2)}, u32[]{:S(2)}) async-start(bf16[32,1,4,384]{3,2,1,0:T(4,128)(2,1)} %bitcast.118), calls=%async_computation.3 | async-start | bytes 196608 | tf_op jit(solution)/shard_map/all_to_all | solution.py:104
  112.2 1.1 copy-start.14
  112.2 1.1 copy-start.21
  113.3 0.9 copy-start.12
  114.2 0.7 copy-start.7
  114.2 1.3 copy-start.9
  116.0 1.6 %copy-start.18 = (f32[32,4]{0,1:T(4,128)S(1)}, f32[32,4]{0,1:T(4,128)}, u32[]{:S(2)}) copy-start(f32[32,4]{0,1:T(4,128)} %add.159) | copy-start | bytes 1540
Sparse Core Ops, SparseCore 0:
  22.9 36.2 all-gather.1
where the time goes:
time: 133 us; the launch traced here: 132 us
  blocking collectives  29.4 us (22%)
  starting transfers between devices  28 us (21%)
  matrix products  23.5 us (18%)
  waiting for transfers between devices  22.3 us (17%)
  between operations  14.2 us (11%)
  local copies, waits for them, and re-layouts  10.5 us (8%)
  other arithmetic  4.24 us (3%)
    all_gather x1, blocking collectives, full_weights(): outp = lax.all_gather(over_gy(w_output), ('gz', 'gx'), axis=2, tiled=True)  22.7 us
    ppermute x6, starting transfers between devices, over_gy(): lax.ppermute(block, 'gy', [(i, (i + s) % ny) for i in range(ny)])  12.3 us
    all_to_all x1, waiting for transfers between devices, from_planes(): return lax.all_to_all(parts, ALL, 0, 0, tiled=True)  7.38 us
    all_to_all x1, waiting for transfers between devices, to_planes(): got = lax.all_to_all(depth_lines, ALL, 0, 0, tiled=True)  7.37 us
    dot_general x6, matrix products, sublayer(): packed = jnp.dot(normed, w_inner, preferred_element_type=jnp.float32)  7.22 us
    all_to_all x1, blocking collectives, local(): return lax.all_to_all(grad_zero, 'gz', 0, 2, tiled=True)  6.67 us
    ppermute x6, waiting for transfers between devices, over_gy(): lax.ppermute(block, 'gy', [(i, (i + s) % ny) for i in range(ny)])  6.16 us
    all_to_all x1, starting transfers between devices, block_to_plane(): got = lax.all_to_all(block, ('gy', 'gx'), 0, 0, tiled=True)  4.9 us
  transfers between devices with their start and end apart: 11, of which 5 were waited for; matrix products, arithmetic and copies ran while one was open for 5% of the time, Pallas kernels for 0%

commit v1 on v0

--- a/solution.py
+++ b/solution.py
@@ -114,7 +114,15 @@
 
 def local(volume, cotangent, w_project, w_output, sizes):
     w_depth, w_row, w_col = full_weights(w_project, w_output, sizes)
-    depth_act = lax.all_to_all(volume, "gz", 2, 0, tiled=True)
+    ways, here = (lax.axis_size("gz"), lax.axis_index("gz"))
+    width = volume.shape[2] // ways
+    turned = jnp.roll(volume, -here * width, axis=2)
+    got_2 = [lax.slice_in_dim(turned, 0, width, axis=2)]
+    for far in range(1, ways):
+        sent = lax.slice_in_dim(turned, far * width, (far + 1) * width, axis=2)
+        got_2.append(lax.ppermute(sent, "gz", [(d, (d + far) % ways) for d in range(ways)]))
+    line = jnp.concatenate(got_2[::-1], axis=0)
+    depth_act = jnp.roll(line, (here + 1) * got_2[0].shape[0], axis=0)
     cot_plane = block_to_plane(cotangent, sizes)
     field_one, depth_pullback = jax.vjp(lambda m: depth_fn(m, *w_depth), depth_act)
     plane_one = to_planes(field_one, sizes)

time: 133 us -> 130 us (0.977)
  starting transfers between devices: 28 us -> 25 us
  matrix products: 23.5 us -> 26.4 us
  blocking collectives: 29.4 us -> 27.5 us
  waiting for transfers between devices: 22.3 us -> 24.1 us
  local copies, waits for them, and re-layouts: 10.5 us -> 9.11 us
    ppermute x0 -> x3, waiting for transfers between devices: none -> 3.8 us  [local(): lax.ppermute(sent, 'gz', [(d, (d + far) % ways) for d in range(ways)])]
    all_to_all x1 -> x0, starting transfers between devices: 3.31 us -> none  [local(): depth_act = lax.all_to_all(volume, 'gz', 2, 0, tiled=True)]
    all_gather x1, blocking collectives: 22.7 us -> 20.9 us  [full_weights(): outp = lax.all_gather(over_gy(w_output), ('gz', 'gx'), axis=2, tiled=True)]
    ppermute x0 -> x3, starting transfers between devices: none -> 1.71 us  [local(): lax.ppermute(sent, 'gz', [(d, (d + far) % ways) for d in range(ways)])]
    unnamed x45 -> x64, local copies, waits for them, and re-layouts: 2.64 us -> 2.84 us
  transfers between devices with their start and end apart: 11 -> 13, of which waited for: 5 -> 5; matrix products, arithmetic and copies ran while one was open for 5% -> 5% of each run, Pallas kernels for 0% -> 0%
where the time goes in v1:
time: 130 us; the launch traced here: 129 us
  blocking collectives  27.5 us (21%)
  matrix products  26.4 us (20%)
  starting transfers between devices  25 us (19%)
  waiting for transfers between devices  24.1 us (19%)
  between operations  14.3 us (11%)
  local copies, waits for them, and re-layouts  9.11 us (7%)
  other arithmetic  3.05 us (2%)
    all_gather x1, blocking collectives, full_weights(): outp = lax.all_gather(over_gy(w_output), ('gz', 'gx'), axis=2, tiled=True)  20.9 us
    ppermute x6, starting transfers between devices, over_gy(): lax.ppermute(block, 'gy', [(i, (i + s) % ny) for i in range(ny)])  12.3 us
    all_to_all x1, waiting for transfers between devices, from_planes(): return lax.all_to_all(parts, ALL, 0, 0, tiled=True)  7.56 us
    dot_general x6, matrix products, sublayer(): packed = jnp.dot(normed, w_inner, preferred_element_type=jnp.float32)  7.27 us
    all_to_all x1, blocking collectives, local(): return lax.all_to_all(grad_zero, 'gz', 0, 2, tiled=True)  6.67 us
    all_to_all x1, waiting for transfers between devices, to_planes(): got = lax.all_to_all(depth_lines, ALL, 0, 0, tiled=True)  6.52 us
    ppermute x6, waiting for transfers between devices, over_gy(): lax.ppermute(block, 'gy', [(i, (i + s) % ny) for i in range(ny)])  6.16 us
    dot_general x12, matrix products, head_norm(): jnp.dot(scale, ones.T, precision=lax.Precision.HIGH)  5.5 us
  transfers between devices with their start and end apart: 13, of which 5 were waited for; matrix products, arithmetic and copies ran while one was open for 5% of the time, Pallas kernels for 0%

profile of v1, /device:TPU:0, one launch (start us, length us, event | category | flops | bytes accessed | tf_op | source)
XLA Modules:
  0.0 129.5 jit_solution(14122426943783696050)
XLA Ops:
  6.5 3.1 %collective-permute-start.6 = (bf16[3,96,144]{1,2,0:T(8,128)(2,1)}, bf16[3,96,144]{1,2,0:T(8,128)(2,1)S(1)}, u32[]{:S(2)}, u32[]{:S(2)}) collective-permute-start(bf16[3,96,144]{1,2,0:T(8,128)(2,1)} %param.6), channel_id=1, source_target_pairs={{0,2},{2,4},{4,6},{6,0},{1,3},{3,5},{5,7},{7,1},{8,10},{10,12},{12... | collective-permute-start | bytes 248840 | tf_op jit(solution)/shard_map/ppermute | solution.py:69
  9.6 2.6 %collective-permute-start.7 = (bf16[3,96,144]{1,2,0:T(8,128)(2,1)}, bf16[3,96,144]{1,2,0:T(8,128)(2,1)S(1)}, u32[]{:S(2)}, u32[]{:S(2)}) collective-permute-start(bf16[3,96,144]{1,2,0:T(8,128)(2,1)} %param.6), channel_id=1, source_target_pairs={{0,4},{2,6},{4,0},{6,2},{1,5},{3,7},{5,1},{7,3},{8,12},{10,14},{12... | collective-permute-start | bytes 248840 | tf_op jit(solution)/shard_map/ppermute | solution.py:69
  12.2 1.3 %collective-permute-start.8 = (bf16[3,96,144]{1,2,0:T(8,128)(2,1)}, bf16[3,96,144]{1,2,0:T(8,128)(2,1)S(1)}, u32[]{:S(2)}, u32[]{:S(2)}) collective-permute-start(bf16[3,96,144]{1,2,0:T(8,128)(2,1)} %param.6), channel_id=1, source_target_pairs={{0,6},{2,0},{4,2},{6,4},{1,7},{3,1},{5,3},{7,5},{8,14},{10,8},{12,... | collective-permute-start | bytes 248840 | tf_op jit(solution)/shard_map/ppermute | solution.py:69
  13.6 2.3 %collective-permute-done.6 = bf16[3,96,144]{1,2,0:T(8,128)(2,1)S(1)} collective-permute-done((bf16[3,96,144]{1,2,0:T(8,128)(2,1)}, bf16[3,96,144]{1,2,0:T(8,128)(2,1)S(1)}, u32[]{:S(2)}, u32[]{:S(2)}) %collective-permute-start.6) | collective-permute-done | bytes 82976 | tf_op jit(solution)/shard_map/ppermute | solution.py:69
  15.8 3.9 %collective-permute-done.7 = bf16[3,96,144]{1,2,0:T(8,128)(2,1)S(1)} collective-permute-done((bf16[3,96,144]{1,2,0:T(8,128)(2,1)}, bf16[3,96,144]{1,2,0:T(8,128)(2,1)S(1)}, u32[]{:S(2)}, u32[]{:S(2)}) %collective-permute-start.7) | collective-permute-done | bytes 82976 | tf_op jit(solution)/shard_map/ppermute | solution.py:69
  19.7 1.0 pad_maximum_fusion
  20.7 0.6 gather_fusion.1
  21.7 1.0 reshape.893
  22.8 2.9 %collective-permute-start = (bf16[3,96,48]{1,2,0:T(8,128)(2,1)S(1)}, bf16[3,96,48]{1,2,0:T(8,128)(2,1)S(1)}, u32[]{:S(2)}, u32[]{:S(2)}) collective-permute-start(bf16[3,96,48]{1,2,0:T(8,128)(2,1)S(1)} %copy-done.17), channel_id=1, source_target_pairs={{0,2},{2,4},{4,6},{6,0},{1,3},{3,5},{5,7},{7,1},{8,10},{10,12},{12... | collective-permute-start | bytes 82952 | tf_op jit(solution)/shard_map/ppermute | solution.py:69
  25.7 1.6 %collective-permute-start.1 = (bf16[3,96,48]{1,2,0:T(8,128)(2,1)S(1)}, bf16[3,96,48]{1,2,0:T(8,128)(2,1)S(1)}, u32[]{:S(2)}, u32[]{:S(2)}) collective-permute-start(bf16[3,96,48]{1,2,0:T(8,128)(2,1)S(1)} %copy-done.17), channel_id=1, source_target_pairs={{0,4},{2,6},{4,0},{6,2},{1,5},{3,7},{5,1},{7,3},{8,12},{10,14},{12... | collective-permute-start | bytes 82952 | tf_op jit(solution)/shard_map/ppermute | solution.py:69
  27.3 0.8 collective-permute-start.2
  28.3 0.6 collective-permute-start.3
  28.9 1.0 collective-permute-start.4
  30.0 4.2 %all-to-all-start = ((bf16[8,1,16,384]{3,2,1,0:T(8,128)(2,1)}), bf16[8,1,16,384]{3,2,1,0:T(8,128)(2,1)S(1)}, u32[]{:S(2)}, u32[]{:S(2)}) async-start(bf16[8,1,16,384]{3,2,1,0:T(8,128)(2,1)} %param.5), calls=%async_computation | async-start | bytes 196608 | tf_op jit(solution)/shard_map/all_to_all | solution.py:110
  34.3 3.8 %collective-permute-done.5 = bf16[8,1,4,384]{3,0,2,1:T(8,128)(2,1)S(1)} collective-permute-done((bf16[8,1,4,384]{3,0,2,1:T(8,128)(2,1)S(1)}, bf16[8,1,4,384]{3,0,2,1:T(8,128)(2,1)S(1)}, u32[]{:S(2)}, u32[]{:S(2)}) %collective-permute-start.5) | collective-permute-done | bytes 24608 | tf_op jit(solution)/shard_map/ppermute | solution.py:123
  38.3 0.5 copy-done.20
  38.9 0.6 gather_fusion
  39.8 20.9 %all_gather.6 = bf16[3,384,384]{1,2,0:T(8,128)(2,1)S(1)} all-gather(bf16[3,384,48]{1,2,0:T(8,128)(2,1)S(1)} %reshape.891), channel_id=1, replica_groups=mesh['gz'=4,'gy'=4,'gx'=2] {'gz','gx'}, dimensions={2}, use_global_device_ids=true | all-gather | bytes 995328 | tf_op jit(solution)/shard_map/all_gather | solution.py:75
  60.7 1.6 %convolution_bitcast_fusion.2 = f32[1,32,4,1152]{3,1,2,0:T(8,128)S(1)} fusion(bf16[3,384,1152]{1,2,0:T(8,128)(2,1)} %all-gather.2.cloned.1.call-done, f32[32,4]{0,1:T(4,128)S(1)} %fusion.322, bf16[64,1,4,384]{3,0,2,1:T(8,128)(2,1)S(1)} %slice_dynamic-update-slice_fusion.1, s32[]{:T(128)S(6)} %select_n.164), kind=kOutput, calls=%fused_computation.4 | convolution fusion | flops 113393664 | bytes 1574916 | tf_op jit(solution)/shard_map/jvp()/dot_general | solution.py:34
  64.7 0.4 fusion.1
  65.4 0.7 copy.23
  66.1 4.2 %all-to-all-start.1 = ((bf16[32,1,4,384]{3,2,1,0:T(4,128)(2,1)}), bf16[32,1,4,384]{3,2,1,0:T(4,128)(2,1)S(1)}, u32[]{:S(2)}, u32[]{:S(2)}) async-start(bf16[32,1,4,384]{3,2,1,0:T(4,128)(2,1)} %copy.23), calls=%async_computation.1 | async-start | bytes 196608 | tf_op jit(solution)/shard_map/all_to_all | solution.py:93
  70.3 0.9 fusion.56
  71.2 6.5 %all-to-all-done.1 = bf16[32,1,4,384]{3,2,1,0:T(4,128)(2,1)S(1)} async-done(((bf16[32,1,4,384]{3,2,1,0:T(4,128)(2,1)}), bf16[32,1,4,384]{3,2,1,0:T(4,128)(2,1)S(1)}, u32[]{:S(2)}, u32[]{:S(2)}) %all-to-all-start.1) | async-done | bytes 98336 | tf_op jit(solution)/shard_map/all_to_all | solution.py:93
  77.9 0.6 multiply_add_fusion
  78.6 1.6 %convolution_bitcast_fusion.1 = f32[1,4,32,1152]{3,2,1,0:T(8,128)S(1)} fusion(bf16[4,32,384]{2,1,0:T(8,128)(2,1)S(1)} %convert_element_type.543, bf16[3,384,1152]{1,2,0:T(8,128)(2,1)} %all-gather.2.cloned.1.call-done), kind=kOutput, calls=%fused_computation.3 | convolution fusion | flops 113246208 | bytes 1572864 | tf_op jit(solution)/shard_map/jvp()/dot_general | solution.py:34
  80.5 0.9 fusion.87
  81.8 1.8 %fusion.208 = (f32[4,32,384]{2,1,0:T(8,128)S(1)}, f32[4,32,384]{2,1,0:T(8,128)S(1)}, f32[4,32,384]{2,1,0:T(8,128)}) fusion(f32[1,4,32,1152]{3,2,1,0:T(8,128)S(1)} %convolution_bitcast_fusion.1, f32[4,32,384]{2,1,0:T(8,128)S(1)} %fusion.247, s32[384]{0:T(512)S(1)} %add_select_fusion, f32[4,32,6]{1,2,0:T(8,128)} %fusion.87), kind=kOutput, calls=%fused_computation.284 | convolution fusion | flops 2066688 | bytes 1184256 | tf_op jit(solution)/shard_map/jvp()/dot_general | solution.py:22
  83.7 0.8 fusion.343
  85.2 0.4 convolution_bitcast_fusion
  87.7 0.7 fusion.129
  90.2 0.4 multiply_reduce_fusion.5
  91.1 0.4 multiply_reduce_fusion.8
  91.6 0.5 multiply_reduce_fusion.1
  92.4 1.0 add_add_fusion.5
  93.4 0.9 fusion.80
  94.3 1.4 %add.181 = f32[4,32]{1,0:T(4,128)} reshape(f32[4,2,4,4]{3,2,1,0:T(4,128)} %get-tuple-element.16) | data formatting | bytes 1024 | tf_op jit(solution)/shard_map/jvp()/add | solution.py:31
  95.6 1.0 add_add_fusion.4
  96.7 1.7 %multiply_reduce_fusion.4 = (f32[4,32]{1,0:T(4,128)S(1)}, f32[4,32,384]{2,1,0:T(8,128)S(1)}) fusion(f32[4,32,384]{2,1,0:T(8,128)S(1)} %reshape.924, bf16[3,384,1152]{1,2,0:T(8,128)(2,1)} %all-gather.2.cloned.1.call-done, f32[1,4,32,384]{3,2,1,0:T(8,128)S(1)} %add_add_fusion.4, f32[1,4,32,384]{3,2,1,0:T(8,128)} %add_add_fusion.5, ...), kind=kOutput, calls=%fused_computation.254 | convolution fusion | flops 113885056 | bytes 1769984 | tf_op jit(solution)/shard_map/transpose(jvp())/dot_general | solution.py:34
  98.5 0.7 copy.29
  99.2 2.6 %all-to-all-start.2 = ((bf16[32,1,4,384]{3,2,1,0:T(4,128)(2,1)}), bf16[32,1,4,384]{3,2,1,0:T(4,128)(2,1)S(1)}, u32[]{:S(2)}, u32[]{:S(2)}) async-start(bf16[32,1,4,384]{3,2,1,0:T(4,128)(2,1)} %bitcast.114), calls=%async_computation.2 | async-start | bytes 196608 | tf_op jit(solution)/shard_map/all_to_all | solution.py:104
  101.8 7.6 %all-to-all-done.2 = bf16[32,1,4,384]{3,2,1,0:T(4,128)(2,1)S(1)} async-done(((bf16[32,1,4,384]{3,2,1,0:T(4,128)(2,1)}), bf16[32,1,4,384]{3,2,1,0:T(4,128)(2,1)S(1)}, u32[]{:S(2)}, u32[]{:S(2)}) %all-to-all-start.2) | async-done | bytes 98336 | tf_op jit(solution)/shard_map/all_to_all | solution.py:104
  109.9 0.7 fusion.125
  111.0 0.5 copy-done.14
  111.8 0.4 copy-done.7
  113.4 1.6 %fusion.167 = (f32[32,4]{0,1:T(4,128)S(1)}, f32[32,4,384]{2,0,1:T(8,128)S(1)}) fusion(bf16[64,1,4,384]{3,0,2,1:T(8,128)(2,1)S(1)} %slice_dynamic-update-slice_fusion.1, s32[]{:T(128)S(6)} %select_n.164, bf16[3,384,1152]{1,2,0:T(8,128)(2,1)} %all-gather.2.cloned.1.call-done, f32[1,32,4,384]{3,1,2,0:T(8,128)S(1)} %add_add_fusion.1, ...), kind=kOutput, calls=%fused_computation.222 | convolution fusion | flops 113934208 | bytes 1671684 | tf_op jit(solution)/shard_map/transpose(jvp())/dot_general | solution.py:34
  115.2 6.7 %all_to_all.33 = bf16[32,1,4,384]{3,2,1,0:T(4,128)(2,1)S(1)} all-to-all(bf16[32,1,4,384]{3,2,1,0:T(4,128)(2,1)S(1)} %copy.32), channel_id=1, replica_groups=mesh['gz'=4,'gy'=4,'gx'=2] {'gz'}, dimensions={0} | all-to-all | bytes 196608 | tf_op jit(solution)/shard_map/all_to_all | solution.py:133
  122.0 0.7 all_to_all.28
  (145 shorter events, 12.5 us)
Async XLA Ops:
  6.5 54.1 %all-gather.2.cloned.1.call-start = ((), (), s32[]{:S(2)}) async-start(), calls=%async_computation.4 | async-start | bytes 2985984 | tf_op jit(solution)/shard_map/all_gather | solution.py:74
  6.5 9.3 %collective-permute-start.6 = (bf16[3,96,144]{1,2,0:T(8,128)(2,1)}, bf16[3,96,144]{1,2,0:T(8,128)(2,1)S(1)}, u32[]{:S(2)}, u32[]{:S(2)}) collective-permute-start(bf16[3,96,144]{1,2,0:T(8,128)(2,1)} %param.6), channel_id=1, source_target_pairs={{0,2},{2,4},{4,6},{6,0},{1,3},{3,5},{5,7},{7,1},{8,10},{10,12},{12... | collective-permute-start | bytes 248840 | tf_op jit(solution)/shard_map/ppermute | solution.py:69
  9.6 10.1 %collective-permute-start.7 = (bf16[3,96,144]{1,2,0:T(8,128)(2,1)}, bf16[3,96,144]{1,2,0:T(8,128)(2,1)S(1)}, u32[]{:S(2)}, u32[]{:S(2)}) collective-permute-start(bf16[3,96,144]{1,2,0:T(8,128)(2,1)} %param.6), channel_id=1, source_target_pairs={{0,4},{2,6},{4,0},{6,2},{1,5},{3,7},{5,1},{7,3},{8,12},{10,14},{12... | collective-permute-start | bytes 248840 | tf_op jit(solution)/shard_map/ppermute | solution.py:69
  12.2 7.5 %collective-permute-start.8 = (bf16[3,96,144]{1,2,0:T(8,128)(2,1)}, bf16[3,96,144]{1,2,0:T(8,128)(2,1)S(1)}, u32[]{:S(2)}, u32[]{:S(2)}) collective-permute-start(bf16[3,96,144]{1,2,0:T(8,128)(2,1)} %param.6), channel_id=1, source_target_pairs={{0,6},{2,0},{4,2},{6,4},{1,7},{3,1},{5,3},{7,5},{8,14},{10,8},{12,... | collective-permute-start | bytes 248840 | tf_op jit(solution)/shard_map/ppermute | solution.py:69
  21.5 1.3 copy-start.17
  21.5 6.6 %copy-start.12 = (bf16[8,1,16,384]{3,2,1,0:T(8,128)(2,1)S(1)}, bf16[8,1,16,384]{3,2,1,0:T(8,128)(2,1)}, u32[]{:S(2)}) copy-start(bf16[8,1,16,384]{3,2,1,0:T(8,128)(2,1)} %param.4) | copy-start | bytes 294916
  22.8 15.5 %collective-permute-start = (bf16[3,96,48]{1,2,0:T(8,128)(2,1)S(1)}, bf16[3,96,48]{1,2,0:T(8,128)(2,1)S(1)}, u32[]{:S(2)}, u32[]{:S(2)}) collective-permute-start(bf16[3,96,48]{1,2,0:T(8,128)(2,1)S(1)} %copy-done.17), channel_id=1, source_target_pairs={{0,2},{2,4},{4,6},{6,0},{1,3},{3,5},{5,7},{7,1},{8,10},{10,12},{12... | collective-permute-start | bytes 82952 | tf_op jit(solution)/shard_map/ppermute | solution.py:69
  25.7 12.7 %collective-permute-start.1 = (bf16[3,96,48]{1,2,0:T(8,128)(2,1)S(1)}, bf16[3,96,48]{1,2,0:T(8,128)(2,1)S(1)}, u32[]{:S(2)}, u32[]{:S(2)}) collective-permute-start(bf16[3,96,48]{1,2,0:T(8,128)(2,1)S(1)} %copy-done.17), channel_id=1, source_target_pairs={{0,4},{2,6},{4,0},{6,2},{1,5},{3,7},{5,1},{7,3},{8,12},{10,14},{12... | collective-permute-start | bytes 82952 | tf_op jit(solution)/shard_map/ppermute | solution.py:69
  27.3 11.0 %collective-permute-start.2 = (bf16[3,96,48]{1,2,0:T(8,128)(2,1)S(1)}, bf16[3,96,48]{1,2,0:T(8,128)(2,1)S(1)}, u32[]{:S(2)}, u32[]{:S(2)}) collective-permute-start(bf16[3,96,48]{1,2,0:T(8,128)(2,1)S(1)} %copy-done.17), channel_id=1, source_target_pairs={{0,6},{2,0},{4,2},{6,4},{1,7},{3,1},{5,3},{7,5},{8,14},{10,8},{12,... | collective-permute-start | bytes 82952 | tf_op jit(solution)/shard_map/ppermute | solution.py:69
  28.3 5.9 %collective-permute-start.3 = (bf16[8,1,4,384]{3,0,2,1:T(8,128)(2,1)S(1)}, bf16[8,1,4,384]{3,0,2,1:T(8,128)(2,1)S(1)}, u32[]{:S(2)}, u32[]{:S(2)}) collective-permute-start(bf16[8,1,4,384]{3,0,2,1:T(8,128)(2,1)S(1)} %get-tuple-element.15), channel_id=1, source_target_pairs={{0,24},{8,0},{16,8},{24,16},{1,25},{9,1},{17,9},{25,17},{2,26},{10... | collective-permute-start | bytes 73736 | tf_op jit(solution)/shard_map/ppermute | solution.py:123
  28.9 5.3 %collective-permute-start.4 = (bf16[8,1,4,384]{3,0,2,1:T(8,128)(2,1)S(1)}, bf16[8,1,4,384]{3,0,2,1:T(8,128)(2,1)S(1)}, u32[]{:S(2)}, u32[]{:S(2)}) collective-permute-start(bf16[8,1,4,384]{3,0,2,1:T(8,128)(2,1)S(1)} %get-tuple-element.14), channel_id=1, source_target_pairs={{0,16},{8,24},{16,0},{24,8},{1,17},{9,25},{17,1},{25,9},{2,18},{10... | collective-permute-start | bytes 73736 | tf_op jit(solution)/shard_map/ppermute | solution.py:123
  30.0 36.1 %all-to-all-start = ((bf16[8,1,16,384]{3,2,1,0:T(8,128)(2,1)}), bf16[8,1,16,384]{3,2,1,0:T(8,128)(2,1)S(1)}, u32[]{:S(2)}, u32[]{:S(2)}) async-start(bf16[8,1,16,384]{3,2,1,0:T(8,128)(2,1)} %param.5), calls=%async_computation | async-start | bytes 196608 | tf_op jit(solution)/shard_map/all_to_all | solution.py:110
  34.2 30.0 %copy-start.25 = (bf16[6,384]{1,0:T(8,128)(2,1)}, bf16[6,384]{1,0:T(8,128)(2,1)S(1)}, u32[]{:S(2)}) copy-start(bf16[6,384]{1,0:T(8,128)(2,1)S(1)} %get-tuple-element.21) | copy-start | bytes 13828
  34.2 3.9 %collective-permute-start.5 = (bf16[8,1,4,384]{3,0,2,1:T(8,128)(2,1)S(1)}, bf16[8,1,4,384]{3,0,2,1:T(8,128)(2,1)S(1)}, u32[]{:S(2)}, u32[]{:S(2)}) collective-permute-start(bf16[8,1,4,384]{3,0,2,1:T(8,128)(2,1)S(1)} %get-tuple-element.13), channel_id=1, source_target_pairs={{0,8},{8,16},{16,24},{24,0},{1,9},{9,17},{17,25},{25,1},{2,10},{10... | collective-permute-start | bytes 73736 | tf_op jit(solution)/shard_map/ppermute | solution.py:123
  38.3 0.6 copy-start.20
  38.3 22.4 %copy-start.18 = (f32[32,4]{0,1:T(4,128)}, f32[32,4]{0,1:T(4,128)S(1)}, u32[]{:S(2)}) copy-start(f32[32,4]{0,1:T(4,128)S(1)} %fusion.322) | copy-start | bytes 1540
  62.6 0.6 copy-start.6
  63.2 0.6 copy-start.10
  64.1 0.6 copy-start.13
  64.1 1.0 copy-start.15
  64.5 0.9 copy-start.3
  64.5 0.9 copy-start.22
  66.1 11.7 %all-to-all-start.1 = ((bf16[32,1,4,384]{3,2,1,0:T(4,128)(2,1)}), bf16[32,1,4,384]{3,2,1,0:T(4,128)(2,1)S(1)}, u32[]{:S(2)}, u32[]{:S(2)}) async-start(bf16[32,1,4,384]{3,2,1,0:T(4,128)(2,1)} %copy.23), calls=%async_computation.1 | async-start | bytes 196608 | tf_op jit(solution)/shard_map/all_to_all | solution.py:93
  80.5 1.0 copy-start.8
  81.8 3.3 %copy-start = (bf16[3,384,1152]{1,2,0:T(8,128)(2,1)S(1)}, bf16[3,384,1152]{1,2,0:T(8,128)(2,1)}, u32[]{:S(2)}) copy-start(bf16[3,384,1152]{1,2,0:T(8,128)(2,1)} %all-gather.2.cloned.1.call-done) | copy-start | bytes 7962628
  85.6 1.2 copy-start.26
  86.5 0.9 copy-start.1
  91.0 1.1 copy-start.9
  91.5 1.8 %copy-start.5 = (f32[4,32,6]{1,2,0:T(8,128)S(1)}, f32[4,32,6]{1,2,0:T(8,128)}, u32[]{:S(2)}) copy-start(f32[4,32,6]{1,2,0:T(8,128)} %fusion.87) | copy-start | bytes 9220
  91.5 4.1 %copy-start.2 = (f32[4,32,384]{2,1,0:T(8,128)S(1)}, f32[4,32,384]{2,1,0:T(8,128)}, u32[]{:S(2)}) copy-start(f32[4,32,384]{2,1,0:T(8,128)} %get-tuple-element.24) | copy-start | bytes 589828
  96.6 1.7 %copy-start.24 = (f32[4,32]{1,0:T(4,128)S(1)}, f32[4,32]{1,0:T(4,128)}, u32[]{:S(2)}) copy-start(f32[4,32]{1,0:T(4,128)} %add.181) | copy-start | bytes 1540
  96.7 5.1 %copy-start.23 = (f32[4,6,32]{2,1,0:T(8,128)S(1)}, f32[4,6,32]{2,1,0:T(8,128)}, u32[]{:S(2)}) copy-start(f32[4,6,32]{2,1,0:T(8,128)} %copy-done.22) | copy-start | bytes 9220
  98.4 11.2 %copy-start.4 = (f32[1,4,6,32,32]{3,4,2,1,0:T(8,128)S(1)}, f32[1,4,6,32,32]{3,4,2,1,0:T(8,128)}, u32[]{:S(2)}) copy-start(f32[1,4,6,32,32]{3,4,2,1,0:T(8,128)} %copy-done.3) | copy-start | bytes 294916
  99.2 10.2 %all-to-all-start.2 = ((bf16[32,1,4,384]{3,2,1,0:T(4,128)(2,1)}), bf16[32,1,4,384]{3,2,1,0:T(4,128)(2,1)S(1)}, u32[]{:S(2)}, u32[]{:S(2)}) async-start(bf16[32,1,4,384]{3,2,1,0:T(4,128)(2,1)} %bitcast.114), calls=%async_computation.2 | async-start | bytes 196608 | tf_op jit(solution)/shard_map/all_to_all | solution.py:104
  109.6 1.1 copy-start.16
  109.6 1.1 copy-start.27
  110.6 0.9 copy-start.14
  111.5 0.7 copy-start.7
  111.5 1.3 copy-start.11
  113.4 1.6 %copy-start.21 = (f32[32,4]{0,1:T(4,128)S(1)}, f32[32,4]{0,1:T(4,128)}, u32[]{:S(2)}) copy-start(f32[32,4]{0,1:T(4,128)} %copy-done.20) | copy-start | bytes 1540
  113.4 1.6 %copy-start.19 = (f32[32,4]{0,1:T(4,128)S(1)}, f32[32,4]{0,1:T(4,128)}, u32[]{:S(2)}) copy-start(f32[32,4]{0,1:T(4,128)} %copy-done.18) | copy-start | bytes 1540
Sparse Core Ops, SparseCore 0:
  22.9 35.3 all-gather.1
